TPU v7x, 128 devices: a whole 4x4x4 slice. The times are simulated.
128 devices in a mesh: ctx: 16 (over z_lo, y, core), ch: 8 (over z_hi, x).
Axes of the slice: x: 4, y: 4, z: 4 (z_hi: 2, z_lo: 2; z = z_hi * 2 + z_lo), core: 2. Of those that a mesh axis runs over, the one named last changes fastest.
Arguments:
- inputs: bfloat16 [512, 512, 1024], P('ctx', None, 'ch'), may hold values from -600 to 600
- norm_gain: float32 [1024], P('ch'), may hold values from 0.1 to 1.9
- conv_taps: float32 [2, 3, 1024], P(None, None, 'ch'), may hold values from -3 to 3
- factor_one: bfloat16 [512, 512], replicated, may hold values from -0.25 to 0.25
- factor_two: bfloat16 [512, 512], replicated, may hold values from -0.25 to 0.25
- kernel: bfloat16 [512, 512, 1024], P(None, 'ctx', 'ch'), may hold values from -5 to 5
- grad_out: bfloat16 [512, 512, 1024], P('ctx', None, 'ch'), may hold values from -5 to 5
Outputs:
- input_grad: bfloat16 [512, 512, 1024], P('ctx', None, 'ch')
- kernel_grad: bfloat16 [512, 512, 1024], P(None, 'ctx', 'ch')
- factor_one_grad: float32 [512, 512], replicated
- factor_two_grad: float32 [512, 512], replicated
- gain_grad: float32 [1024], P('ch')
- taps_grad: float32 [2, 3, 1024], P(None, None, 'ch')
All inputs are finite; a program needn't handle non-finite values.
Results may differ from a plain program's by a relative error of at most 0.0081.
Values may be sent and summed in bfloat16 or wider, within the bound.
No kernel may reach another device: no remote copies, remote signals or barrier semaphores. Data moves between devices by JAX's collectives and lax.ppermute only.
A program may use at most 192 MiB of HBM per device.

v0:
```python
import math
import jax
import jax.numpy as jnp
from jax import lax
from jax.sharding import PartitionSpec as P

OUTER = 512
INNER = 512
WIDTH = 1024


def shifted(value, axis, steps):
    count = lax.axis_size(axis)
    initial, last = (max(0, -steps), min(count, count - steps))
    return lax.ppermute(value, axis, [(source, source + steps) for source in range(initial, last)])


def tree_psum(value, axis):
    count = lax.axis_size(axis)
    step = 1
    while step < count:
        pairs = [(source, source ^ step) for source in range(count)]
        value = jax.tree.map(lambda v, r: v + r, value, lax.ppermute(value, axis, pairs))
        step *= 2
    return value


def on_device(inputs, norm_gain, conv_taps, factor_one, factor_two, kernel, grad_out):
    local_outer, inner, chans = inputs.shape
    rows = local_outer * inner
    taps_count = conv_taps.shape[1]
    flat_in = inputs.reshape(rows, chans).astype(jnp.float32)
    squares = tree_psum(jnp.sum(flat_in * flat_in, axis=1), "ch")
    inverse = lax.rsqrt(squares / WIDTH + 1e-05)
    hat = flat_in * inverse[:, None]
    normed = (hat * norm_gain).astype(jnp.bfloat16)
    earlier = shifted(normed[rows - (taps_count - 1) :], "ctx", 1)
    extended = jnp.concatenate([earlier, normed], 0)
    value_pre = jnp.zeros((rows, chans), jnp.float32)
    gate_pre = jnp.zeros((rows, chans), jnp.float32)
    for offset in range(taps_count):
        window = extended[taps_count - 1 - offset : taps_count - 1 - offset + rows]
        value_pre = value_pre + conv_taps[0, offset] * window
        gate_pre = gate_pre + conv_taps[1, offset] * window
    mixed_in = value_pre.astype(jnp.bfloat16).reshape(local_outer, inner, chans)
    gate = jax.nn.sigmoid(gate_pre)
    cotangent = grad_out.reshape(rows, chans).astype(jnp.float32)
    section_one = jnp.einsum(
        "ijc,jk->ikc", mixed_in, factor_one, preferred_element_type=jnp.float32
    ).astype(jnp.bfloat16)
    out_grad = (cotangent * gate).astype(jnp.bfloat16).reshape(local_outer, inner, chans)
    columns = lax.all_to_all(section_one, "ctx", split_axis=1, concat_axis=0, tiled=True)
    kern = kernel.astype(jnp.float32)
    spectrum = (columns.astype(jnp.float32) * kern).astype(jnp.bfloat16)
    section_two = jnp.einsum(
        "ijc,ik->kjc", spectrum, factor_two, preferred_element_type=jnp.float32
    ).astype(jnp.bfloat16)
    back_rows = lax.all_to_all(section_two, "ctx", split_axis=0, concat_axis=1, tiled=True)
    grad_columns = lax.all_to_all(out_grad, "ctx", split_axis=1, concat_axis=0, tiled=True)
    grad_spec = jnp.einsum(
        "kjc,ik->ijc", grad_columns, factor_two, preferred_element_type=jnp.float32
    )
    kernel_grad = (grad_spec * columns.astype(jnp.float32)).astype(jnp.bfloat16)
    grad_section = (grad_spec * kern).astype(jnp.bfloat16)
    two_part = jnp.einsum("ijc,kjc->ik", spectrum, grad_columns, preferred_element_type=jnp.float32)
    two_total = lax.psum(two_part, ("ctx", "ch"))
    grad_rows = lax.all_to_all(grad_section, "ctx", split_axis=0, concat_axis=1, tiled=True)
    back_flat = back_rows.reshape(rows, chans).astype(jnp.float32)
    grad_gate_pre = cotangent * back_flat * gate * (1.0 - gate)
    grad_mixed = jnp.einsum(
        "ikc,jk->ijc", grad_rows, factor_one, preferred_element_type=jnp.float32
    ).reshape(rows, chans)
    one_part = jnp.einsum("ijc,ikc->jk", mixed_in, grad_rows, preferred_element_type=jnp.float32)
    two_total, one_part = lax.optimization_barrier((two_total, one_part))
    one_total = lax.psum(one_part, ("ctx", "ch"))
    later_value, later_gate = shifted(
        (grad_mixed[: taps_count - 1], grad_gate_pre[: taps_count - 1]), "ctx", -1
    )
    ext_value = jnp.concatenate([grad_mixed, later_value], 0)
    ext_gate = jnp.concatenate([grad_gate_pre, later_gate], 0)
    grad_normed = jnp.zeros((rows, chans), jnp.float32)
    value_taps = []
    gate_taps = []
    for offset in range(taps_count):
        grad_normed = grad_normed + conv_taps[0, offset] * ext_value[offset : offset + rows]
        grad_normed = grad_normed + conv_taps[1, offset] * ext_gate[offset : offset + rows]
        window = extended[taps_count - 1 - offset : taps_count - 1 - offset + rows]
        value_taps.append(jnp.sum(grad_mixed * window, axis=0))
        gate_taps.append(jnp.sum(grad_gate_pre * window, axis=0))
    tap_part = jnp.stack([jnp.stack(value_taps), jnp.stack(gate_taps)])
    gain_part = jnp.sum(grad_normed * hat, axis=0)
    gain_total, taps_total = tree_psum((gain_part, tap_part), "ctx")
    scaled = grad_normed * norm_gain
    row_mean = tree_psum(jnp.sum(scaled * hat, axis=1), "ch") / WIDTH
    input_grad = (
        (inverse[:, None] * (scaled - hat * row_mean[:, None]))
        .astype(jnp.bfloat16)
        .reshape(local_outer, inner, chans)
    )
    seq_scale = 1.0 / math.sqrt(OUTER * INNER)
    factor_one_grad = one_total / math.sqrt(OUTER * WIDTH)
    factor_two_grad = two_total / math.sqrt(INNER * WIDTH)
    return (
        input_grad,
        kernel_grad,
        factor_one_grad,
        factor_two_grad,
        gain_total * seq_scale,
        taps_total * seq_scale,
    )


def solution(mesh):
    in_specs = (
        P("ctx", None, "ch"),
        P("ch"),
        P(None, None, "ch"),
        P(),
        P(),
        P(None, "ctx", "ch"),
        P("ctx", None, "ch"),
    )
    out_specs = (P("ctx", None, "ch"), P(None, "ctx", "ch"), P(), P(), P("ch"), P(None, None, "ch"))
    return jax.shard_map(
        on_device, mesh=mesh, in_specs=in_specs, out_specs=out_specs, check_vma=False
    )
```

profile of v0, /device:TPU:1, one launch (start us, length us, event | category | flops | bytes accessed | tf_op | source)
XLA Modules:
  0.0 703.5 jit_solution(7908504238556587428)
XLA Ops:
  7.2 6.5 copy.43
  13.7 3.1 multiply_reduce_fusion.3
  16.8 2.1 collective-permute-start
  20.6 3.1 collective-permute-start.1
  25.3 3.9 collective-permute-start.2
  29.2 7.1 %copy.44 = f32[32,512,128]{2,1,0:T(8,128)} copy(bf16[32,512,128]{1,2,0:T(8,128)(2,1)} %copy.43) | data formatting | bytes 12582912 | tf_op jit(solution)/shard_map/convert_element_type | solution.py:32
  36.3 5.5 multiply_convert_fusion.2
  41.8 6.3 collective-permute-start.3
  48.9 6.5 fusion.10
  55.4 3.0 fusion.21
  60.4 4.5 convert_bitcast_fusion.3
  64.9 8.0 %copy.55 = bf16[32,512,128]{2,0,1:T(8,128)(2,1)} copy(bf16[32,512,128]{1,2,0:T(8,128)(2,1)} %convert_bitcast_fusion.3) | data formatting | bytes 8388608 | tf_op jit(solution)/shard_map/convert_element_type | solution.py:50
  72.9 6.4 all-to-all-start.2
  79.2 6.9 copy.45
  86.1 48.8 %all-to-all-done.2 = bf16[32,512,128]{2,0,1:T(8,128)(2,1)} async-done(((bf16[32,512,128]{2,0,1:T(8,128)(2,1)}), bf16[32,512,128]{2,0,1:T(8,128)(2,1)}, u32[]{:S(2)}, u32[]{:S(2)}) %all-to-all-start.2) | async-done | bytes 4194336 | tf_op jit(solution)/shard_map/all_to_all | solution.py:52
  134.9 4.9 all-to-all-start
  139.8 7.5 %copy.49 = bf16[512,32,128]{0,2,1:T(8,128)(2,1)} copy(bf16[512,32,128]{2,1,0:T(8,128)(2,1)} %param.12) | data formatting | bytes 8388608 | tf_op args[5]
  147.3 3.8 copy.56
  152.3 4.3 copy.57
  156.6 9.9 %copy.58 = f32[512,32,128]{0,2,1:T(8,128)} copy(f32[512,32,128]{2,1,0:T(8,128)} %bitcast.104) | data formatting | bytes 16777216 | tf_op jit(solution)/shard_map/convert_element_type | solution.py:54
  166.6 8.9 %convert_bitcast_fusion.2 = bf16[512,32,128]{0,2,1:T(8,128)(2,1)} fusion(bf16[512,512]{1,0:T(8,128)(2,1)S(1)} %copy-done, f32[512,32,128]{0,2,1:T(8,128)} %copy.58, bf16[512,32,128]{0,2,1:T(8,128)(2,1)} %copy.49), kind=kOutput, calls=%fused_computation.66 | convolution fusion | flops 2155872256 | bytes 17301504 | tf_op jit(solution)/shard_map/ijc,ik->kjc/dot_general | solution.py:55
  175.5 7.9 %copy.59 = bf16[512,32,128]{2,1,0:T(8,128)(2,1)} copy(bf16[512,32,128]{0,2,1:T(8,128)(2,1)} %convert_bitcast_fusion.2) | data formatting | bytes 8388608 | tf_op jit(solution)/shard_map/convert_element_type | solution.py:57
  183.4 12.1 %all-to-all-done = bf16[32,512,128]{2,0,1:T(8,128)(2,1)} async-done(((bf16[32,512,128]{2,0,1:T(8,128)(2,1)}), bf16[32,512,128]{2,0,1:T(8,128)(2,1)}, u32[]{:S(2)}, u32[]{:S(2)}) %all-to-all-start) | async-done | bytes 4194336 | tf_op jit(solution)/shard_map/all_to_all | solution.py:59
  195.5 5.1 all-to-all-start.3
  200.6 4.1 copy.47
  204.8 12.5 %fusion.29 = (bf16[512,32,128]{0,2,1:T(8,128)(2,1)}, bf16[512,32,128]{0,2,1:T(8,128)(2,1)}) fusion(f32[512,32,128]{0,2,1:T(8,128)} %copy.58, bf16[512,32,128]{0,2,1:T(8,128)(2,1)S(1)} %copy-done.3, bf16[512,512]{1,0:T(8,128)(2,1)S(1)} %copy-done, bf16[512,32,128]{2,1,0:T(8,128)(2,1)S(1)} %bitcast.102), kind=kOutput, calls=%fused_computation.53 | convolution fusion | flops 2157969408 | bytes 25690112 | tf_op jit(solution)/shard_map/kjc,ik->ijc/dot_general | solution.py:60
  217.3 7.9 %copy.50 = bf16[512,32,128]{2,1,0:T(8,128)(2,1)} copy(bf16[512,32,128]{0,2,1:T(8,128)(2,1)} %get-tuple-element.42) | data formatting | bytes 8388608 | tf_op jit(solution)/shard_map/convert_element_type | solution.py:64
  225.2 31.3 %all-to-all-done.3 = bf16[512,32,128]{2,1,0:T(8,128)(2,1)} async-done(((bf16[512,32,128]{2,1,0:T(8,128)(2,1)}), bf16[512,32,128]{2,1,0:T(8,128)(2,1)}, u32[]{:S(2)}, u32[]{:S(2)}) %all-to-all-start.3) | async-done | bytes 4194336 | tf_op jit(solution)/shard_map/all_to_all | solution.py:58
  256.5 4.9 all-to-all-start.1
  261.8 3.4 convert_bitcast_fusion
  265.2 4.3 copy.60
  269.5 47.6 %all-to-all-done.1 = bf16[512,32,128]{2,1,0:T(8,128)(2,1)} async-done(((bf16[512,32,128]{2,1,0:T(8,128)(2,1)}), bf16[512,32,128]{2,1,0:T(8,128)(2,1)}, u32[]{:S(2)}, u32[]{:S(2)}) %all-to-all-start.1) | async-done | bytes 4194336 | tf_op jit(solution)/shard_map/all_to_all | solution.py:67
  317.1 3.6 copy.51
  320.7 7.0 multiply_reduce_fusion
  327.7 9.0 %copy.53 = f32[32,512,128]{2,1,0:T(8,128)} copy(f32[32,512,128]{1,2,0:T(8,128)} %get-tuple-element.50) | data formatting | bytes 16777216 | tf_op jit(solution)/shard_map/ikc,jk->ijc/transpose | solution.py:70
  337.3 14.0 %fusion.22 = (f32[128]{0:T(128)S(1)}, f32[128]{0:T(128)S(1)}, f32[128]{0:T(128)S(1)}, f32[128]{0:T(128)S(1)}, f32[128]{0:T(128)S(1)}, /*index=5*/f32[16384,128]{1,0:T(8,128)S(1)}) fusion(bf16[16384,128]{1,0:T(8,128)(2,1)} %copy-done.4, bf16[2,128]{1,0:T(2,128)(2,1)S(1)} %collective-permute-done.3, bf16[16384,128]{1,0:T(8,128)(2,1)} %copy-done.7, ...), kind=kLoop, calls=%fused_computation.41 | loop fusion | flops 60816768 | bytes 37753344 | tf_op jit(solution)/shard_map/reduce_sum | solution.py:89
  351.3 2.6 collective-permute-start.5
  359.2 24.3 %multiply_reduce_fusion.1 = (f32[128]{0:T(128)S(1)}, f32[16384]{0:T(1024)S(1)}, f32[16384,128]{1,0:T(8,128)}) fusion(f32[32,512,128]{2,1,0:T(8,128)} %copy.44, f32[16384]{0:T(1024)S(1)} %add_rsqrt_fusion, f32[128]{0:T(128)S(1)} %copy-done.13, f32[2,128]{1,0:T(2,128)S(1)} %collective-permute-done.5, f32[16384,128]{1,0:T(8,128)} %copy-done.8, ...), kind=kLoop, calls=%fused_computation.57 | loop fusion | flops 44023680 | bytes 33691648 | tf_op jit(solution)/shard_map/reduce_sum | solution.py:91
  386.7 8.7 %fusion.35 = f32[512,512]{1,0:T(8,128)} fusion(bf16[512,32,128]{2,1,0:T(8,128)(2,1)} %bitcast.103, f32[512,32,128]{0,2,1:T(8,128)S(1)} %bitcast.99, bf16[512,32,128]{0,2,1:T(8,128)(2,1)} %copy.49), kind=kOutput, calls=%fused_computation.73 | convolution fusion | flops 2153775104 | bytes 17825792 | tf_op jit(solution)/shard_map/ijc,kjc->ik/dot_general | solution.py:65
  395.4 7.9 %copy.64 = bf16[512,32,128]{2,1,0:T(8,128)(2,1)} copy(bf16[512,32,128]{0,2,1:T(8,128)(2,1)} %get-tuple-element.41) | data formatting | bytes 8388608
  404.7 6.8 convolution_bitcast_fusion.1
  411.6 130.2 %all-reduce.3.cloned.1.call-done = f32[512,512]{1,0:T(8,128)} async-done(((f32[512,512]{1,0:T(8,128)}), f32[512,512]{1,0:T(8,128)}) %all-reduce.3.cloned.1.call-update) | async-done | bytes 1048592 | tf_op jit(solution)/shard_map/psum | solution.py:66
  544.8 2.3 broadcast_multiply_fusion
  550.8 2.1 collective-permute-done.7
  552.9 2.4 collective-permute-start.8
  557.9 11.5 %multiply_convert_fusion.1 = bf16[16384,128]{1,0:T(8,128)(2,1)} fusion(f32[16384,128]{1,0:T(8,128)} %get-tuple-element.38, f32[32,512,128]{2,1,0:T(8,128)} %copy.44, f32[16384]{0:T(1024)S(1)} %add_multiply_fusion, f32[128]{0:T(128)S(1)} %copy-done.13, f32[16384]{0:T(1024)S(1)} %add_rsqrt_fusion), kind=kLoop, calls=%fused_computation.58 | loop fusion | flops 12582912 | bytes 21103104 | tf_op jit(solution)/shard_map/convert_element_type | solution.py:97
  569.5 124.7 %all-reduce.5.cloned.1.call-done = f32[512,512]{1,0:T(8,128)} async-done(((f32[512,512]{1,0:T(8,128)}), f32[512,512]{1,0:T(8,128)}) %all-reduce.5.cloned.1.call-update) | async-done | bytes 1048592 | tf_op jit(solution)/shard_map/psum | solution.py:75
  694.1 2.3 broadcast_multiply_fusion.1
  (90 shorter events, 27.5 us)
Async XLA Ops:
  7.2 159.4 %copy-start = (bf16[512,512]{1,0:T(8,128)(2,1)S(1)}, bf16[512,512]{1,0:T(8,128)(2,1)}, u32[]{:S(2)}) copy-start(bf16[512,512]{1,0:T(8,128)(2,1)} %param.11) | copy-start | bytes 1572868
  13.7 22.7 %copy-start.13 = (f32[128]{0:T(128)S(1)}, f32[128]{0:T(128)}, u32[]{:S(2)}) copy-start(f32[128]{0:T(128)} %param.8) | copy-start | bytes 1540
  16.8 3.8 collective-permute-start
  20.6 4.7 collective-permute-start.1
  25.3 11.0 %collective-permute-start.2 = (f32[16384]{0:T(1024)S(1)}, f32[16384]{0:T(1024)S(1)}, u32[]{:S(2)}, u32[]{:S(2)}) collective-permute-start(f32[16384]{0:T(1024)S(1)} %add.83), channel_id=1, source_target_pairs={{0,4},{1,5},{2,6},{3,7},{4,0},{5,1},{6,2},{7,3},{8,12},{9,13},{10,... | collective-permute-start | bytes 196616 | tf_op jit(solution)/shard_map/ppermute | solution.py:23
  36.3 11.9 %copy-start.14 = (f32[2,3,128]{2,0,1:T(2,128)S(1)}, f32[2,3,128]{2,0,1:T(2,128)}, u32[]{:S(2)}) copy-start(f32[2,3,128]{2,0,1:T(2,128)} %param.9) | copy-start | bytes 9220
  36.3 12.6 %copy-start.10 = (bf16[32,512,128]{2,1,0:T(8,128)(2,1)S(1)}, bf16[32,512,128]{2,1,0:T(8,128)(2,1)}, u32[]{:S(2)}) copy-start(bf16[32,512,128]{2,1,0:T(8,128)(2,1)} %param.13) | copy-start | bytes 12582916
  41.8 13.6 %copy-start.4 = (bf16[16384,128]{1,0:T(8,128)(2,1)}, bf16[16384,128]{1,0:T(8,128)(2,1)S(1)}, u32[]{:S(2)}) copy-start(bf16[16384,128]{1,0:T(8,128)(2,1)S(1)} %multiply_convert_fusion.2) | copy-start | bytes 12582916
  41.8 7.1 %collective-permute-start.3 = (bf16[2,128]{1,0:T(2,128)(2,1)S(1)}, bf16[2,128]{1,0:T(2,128)(2,1)S(1)}, u32[]{:S(2)}, u32[]{:S(2)}) collective-permute-start(bf16[2,128]{1,0:T(2,128)(2,1)S(1)} %slice.68), channel_id=1, source_target_pairs={{0,8},{8,16},{16,24},{24,32},{32,40},{40,48},{48,56},{56,64},{64,7... | collective-permute-start | bytes 1544 | tf_op jit(solution)/shard_map/ppermute | solution.py:15
  55.4 3.0 copy-start.7
  55.4 5.0 copy-start.12
  58.4 1.9 copy-start.9
  72.9 62.0 %all-to-all-start.2 = ((bf16[32,512,128]{2,0,1:T(8,128)(2,1)}), bf16[32,512,128]{2,0,1:T(8,128)(2,1)}, u32[]{:S(2)}, u32[]{:S(2)}) async-start(bf16[32,512,128]{2,0,1:T(8,128)(2,1)} %copy.55), calls=%async_computation.2 | async-start | bytes 8388608 | tf_op jit(solution)/shard_map/all_to_all | solution.py:52
  134.9 60.6 %all-to-all-start = ((bf16[32,512,128]{2,0,1:T(8,128)(2,1)}), bf16[32,512,128]{2,0,1:T(8,128)(2,1)}, u32[]{:S(2)}, u32[]{:S(2)}) async-start(bf16[32,512,128]{2,0,1:T(8,128)(2,1)} %copy.45), calls=%async_computation | async-start | bytes 8388608 | tf_op jit(solution)/shard_map/all_to_all | solution.py:59
  195.5 61.0 %all-to-all-start.3 = ((bf16[512,32,128]{2,1,0:T(8,128)(2,1)}), bf16[512,32,128]{2,1,0:T(8,128)(2,1)}, u32[]{:S(2)}, u32[]{:S(2)}) async-start(bf16[512,32,128]{2,1,0:T(8,128)(2,1)} %copy.59), calls=%async_computation.3 | async-start | bytes 8388608 | tf_op jit(solution)/shard_map/all_to_all | solution.py:58
  200.6 4.1 copy-start.3
  204.7 12.6 %copy-start.5 = (bf16[16,32,32,128]{3,2,1,0:T(8,128)(2,1)}, bf16[16,32,32,128]{3,2,1,0:T(8,128)(2,1)S(1)}, u32[]{:S(2)}) copy-start(bf16[16,32,32,128]{3,2,1,0:T(8,128)(2,1)S(1)} %copy.47) | copy-start | bytes 12582916
  256.5 60.6 %all-to-all-start.1 = ((bf16[512,32,128]{2,1,0:T(8,128)(2,1)}), bf16[512,32,128]{2,1,0:T(8,128)(2,1)}, u32[]{:S(2)}, u32[]{:S(2)}) async-start(bf16[512,32,128]{2,1,0:T(8,128)(2,1)} %copy.50), calls=%async_computation.1 | async-start | bytes 8388608 | tf_op jit(solution)/shard_map/all_to_all | solution.py:67
  261.4 280.4 %all-reduce.3.cloned.1.call-start = ((), (), s32[]{:S(2)}) async-start(), calls=%async_computation.4 | async-start | bytes 2097152 | tf_op jit(solution)/shard_map/psum | solution.py:66
  317.1 3.6 copy-start.6
  320.7 7.1 %copy-start.11 = (bf16[32,16,32,128]{3,2,1,0:T(8,128)(2,1)}, bf16[32,16,32,128]{3,2,1,0:T(8,128)(2,1)S(1)}, u32[]{:S(2)}) copy-start(bf16[32,16,32,128]{3,2,1,0:T(8,128)(2,1)S(1)} %copy.51) | copy-start | bytes 12582916
  337.3 21.9 %copy-start.2 = (f32[32,512,128]{2,1,0:T(8,128)S(1)}, f32[32,512,128]{2,1,0:T(8,128)}, u32[]{:S(2)}) copy-start(f32[32,512,128]{2,1,0:T(8,128)} %copy.53) | copy-start | bytes 25165828
  351.3 4.6 copy-start.8
  351.3 5.9 collective-permute-start.5
  353.9 5.3 collective-permute-start.4
  355.9 30.8 %slice-start = ((s8[8388608]{0:T(1024)(128)(4,1)}), s8[4194304]{0:T(1024)(128)(4,1)S(1)}, s32[]{:S(2)}) async-start(s8[8388608]{0:T(1024)(128)(4,1)} %bitcast.98), calls=%async_computation.6 | async-start | bytes 8388608
  355.9 30.8 %slice-start.1 = ((s8[8388608]{0:T(1024)(128)(4,1)}), s8[4194304]{0:T(1024)(128)(4,1)S(1)}, s32[]{:S(2)}) async-start(s8[8388608]{0:T(1024)(128)(4,1)} %bitcast.98), calls=%async_computation.7 | async-start | bytes 8388608
  383.5 1.2 collective-permute-start.9
  383.6 21.1 %collective-permute-start.13 = (f32[2,3,128]{2,1,0:T(4,128)S(1)}, f32[2,3,128]{2,1,0:T(4,128)S(1)}, u32[]{:S(2)}, u32[]{:S(2)}) collective-permute-start(f32[2,3,128]{2,1,0:T(4,128)S(1)} %pad_maximum_fusion.3), channel_id=1, source_target_pairs={{0,8},{8,0},{16,24},{24,16},{32,40},{40,32},{48,56},{56,48},{64,72... | collective-permute-start | bytes 9224 | tf_op jit(solution)/shard_map/ppermute | solution.py:23
  384.7 18.6 %collective-permute-start.10 = (f32[128]{0:T(128)S(1)}, f32[128]{0:T(128)S(1)}, u32[]{:S(2)}, u32[]{:S(2)}) collective-permute-start(f32[128]{0:T(128)S(1)} %add.100), channel_id=1, source_target_pairs={{0,16},{8,24},{16,0},{24,8},{32,48},{40,56},{48,32},{56,40},{64,80... | collective-permute-start | bytes 1544 | tf_op jit(solution)/shard_map/ppermute | solution.py:23
  395.4 298.7 %all-reduce.5.cloned.1.call-start = ((), (), s32[]{:S(2)}) async-start(), calls=%async_computation.5 | async-start | bytes 2097152 | tf_op jit(solution)/shard_map/psum | solution.py:75
  403.3 138.9 %collective-permute-start.11 = (f32[128]{0:T(128)S(1)}, f32[128]{0:T(128)S(1)}, u32[]{:S(2)}, u32[]{:S(2)}) collective-permute-start(f32[128]{0:T(128)S(1)} %add.101), channel_id=1, source_target_pairs={{0,32},{8,40},{16,48},{24,56},{32,0},{40,8},{48,16},{56,24},{64,96... | collective-permute-start | bytes 1544 | tf_op jit(solution)/shard_map/ppermute | solution.py:23
  404.6 138.4 %collective-permute-start.14 = (f32[2,3,128]{2,1,0:T(4,128)S(1)}, f32[2,3,128]{2,1,0:T(4,128)S(1)}, u32[]{:S(2)}, u32[]{:S(2)}) collective-permute-start(f32[2,3,128]{2,1,0:T(4,128)S(1)} %fusion.42), channel_id=1, source_target_pairs={{0,16},{8,24},{16,0},{24,8},{32,48},{40,56},{48,32},{56,40},{64,80... | collective-permute-start | bytes 9224 | tf_op jit(solution)/shard_map/ppermute | solution.py:23
  541.7 6.5 collective-permute-start.6
  542.2 8.1 %collective-permute-start.12 = (f32[128]{0:T(128)S(1)}, f32[128]{0:T(128)S(1)}, u32[]{:S(2)}, u32[]{:S(2)}) collective-permute-start(f32[128]{0:T(128)S(1)} %add.102), channel_id=1, source_target_pairs={{0,64},{8,72},{16,80},{24,88},{32,96},{40,104},{48,112},{56,120},{... | collective-permute-start | bytes 1544 | tf_op jit(solution)/shard_map/ppermute | solution.py:23
  543.1 4.0 collective-permute-start.15
  547.1 8.2 %collective-permute-start.16 = (f32[2,3,128]{2,1,0:T(4,128)S(1)}, f32[2,3,128]{2,1,0:T(4,128)S(1)}, u32[]{:S(2)}, u32[]{:S(2)}) collective-permute-start(f32[2,3,128]{2,1,0:T(4,128)S(1)} %add.106), channel_id=1, source_target_pairs={{0,64},{8,72},{16,80},{24,88},{32,96},{40,104},{48,112},{56,120},{... | collective-permute-start | bytes 9224 | tf_op jit(solution)/shard_map/ppermute | solution.py:23
  548.2 4.7 collective-permute-start.7
  552.9 5.0 collective-permute-start.8
  557.9 138.5 %copy-start.1 = (bf16[512,512]{1,0:T(8,128)(2,1)S(1)}, bf16[512,512]{1,0:T(8,128)(2,1)}, u32[]{:S(2)}) copy-start(bf16[512,512]{1,0:T(8,128)(2,1)} %param.11) | copy-start | bytes 1572868
Sparse Core Ops, SparseCore 0:
  395.5 146.1 all-reduce.2
  547.1 147.0 all-reduce.4
where the time goes:
time: 712 us; the launch traced here: 703 us
  waiting for transfers between devices  407 us (57%)
  local copies, waits for them, and re-layouts  102 us (14%)
  other arithmetic  77.7 us (11%)
  starting transfers between devices  54 us (8%)
  matrix products  48.5 us (7%)
  between operations  14.6 us (2%)
    psum x1, waiting for transfers between devices, on_device(): two_total = lax.psum(two_part, ('ctx', 'ch'))  130 us
    psum x1, waiting for transfers between devices, on_device(): one_total = lax.psum(one_part, ('ctx', 'ch'))  125 us
    all_to_all x1, waiting for transfers between devices, on_device(): lax.all_to_all(section_one, 'ctx', split_axis=1, concat_axis=0, tiled=True)  48.8 us
    all_to_all x1, waiting for transfers between devices, on_device(): lax.all_to_all(grad_section, 'ctx', split_axis=0, concat_axis=1, tiled=True)  47.6 us
    all_to_all x1, waiting for transfers between devices, on_device(): lax.all_to_all(section_two, 'ctx', split_axis=0, concat_axis=1, tiled=True)  31.3 us
    unnamed x39, local copies, waits for them, and re-layouts  24.5 us
    reduce_sum x1, other arithmetic, on_device(): gain_part = jnp.sum(grad_normed * hat, axis=0)  24.3 us
    ppermute x14, starting transfers between devices, tree_psum(): lax.ppermute(value, axis, pairs)  21.5 us
  transfers between devices with their start and end apart: 23, of which 15 were waited for; matrix products, arithmetic and copies ran while one was open for 18% of the time, Pallas kernels for 0%

commit v1 on v0

--- a/solution.py
+++ b/solution.py
@@ -64,7 +64,12 @@
     grad_section = (grad_spec * kern).astype(jnp.bfloat16)
     two_part = jnp.einsum("ijc,kjc->ik", spectrum, grad_columns, preferred_element_type=jnp.float32)
     two_total = lax.psum(two_part, ("ctx", "ch"))
-    grad_rows = lax.all_to_all(grad_section, "ctx", split_axis=0, concat_axis=1, tiled=True)
+    grad_rows = jnp.concatenate(
+        lax.all_to_all(
+            jnp.stack(jnp.split(grad_section, lax.axis_size("ctx"), axis=0)), "ctx", 0, 0
+        ),
+        axis=1,
+    )
     back_flat = back_rows.reshape(rows, chans).astype(jnp.float32)
     grad_gate_pre = cotangent * back_flat * gate * (1.0 - gate)
     grad_mixed = jnp.einsum(

time: 712 us -> 735 us (1.032)
  local copies, waits for them, and re-layouts: 102 us -> 154 us
  waiting for transfers between devices: 407 us -> 376 us
    another operation x0 -> x18, local copies, waits for them, and re-layouts: none -> 39.9 us  [on_device(): jnp.stack(jnp.split(grad_section, lax.axis_size('ctx'), axis=0))]
    all_to_all x1, waiting for transfers between devices: 31.3 us -> 0.01 us  [on_device(): lax.all_to_all(section_two, 'ctx', split_axis=0, concat_axis=1, tiled=True)]
    unnamed x39 -> x56, local copies, waits for them, and re-layouts: 24.5 us -> 44.9 us
    convert_element_type x1 -> x0, local copies, waits for them, and re-layouts: 7.89 us -> none  [on_device(): grad_section = (grad_spec * kern).astype(jnp.bfloat16)]
  transfers between devices with their start and end apart: 23 -> 23, of which waited for: 15 -> 14; matrix products, arithmetic and copies ran while one was open for 18% -> 25% of each run, Pallas kernels for 0% -> 0%
where the time goes in v1:
time: 735 us; the launch traced here: 725 us
  waiting for transfers between devices  376 us (51%)
  local copies, waits for them, and re-layouts  154 us (21%)
  other arithmetic  77.8 us (11%)
  starting transfers between devices  54.9 us (7%)
  matrix products  47.9 us (7%)
  between operations  14.7 us (2%)
    psum x1, waiting for transfers between devices, on_device(): two_total = lax.psum(two_part, ('ctx', 'ch'))  130 us
    psum x1, waiting for transfers between devices, on_device(): one_total = lax.psum(one_part, ('ctx', 'ch'))  125 us
    all_to_all x1, waiting for transfers between devices, on_device(): lax.all_to_all(section_one, 'ctx', split_axis=1, concat_axis=0, tiled=True)  48.8 us
    all_to_all x1, waiting for transfers between devices, on_device(): lax.all_to_all(jnp.stack(jnp.split(grad_section, lax.axis_size('ctx'), ax...  47.9 us
    unnamed x56, local copies, waits for them, and re-layouts  44.9 us
    another operation x18, local copies, waits for them, and re-layouts, on_device(): jnp.stack(jnp.split(grad_section, lax.axis_size('ctx'), axis=0))  39.9 us
    reduce_sum x1, other arithmetic, on_device(): gain_part = jnp.sum(grad_normed * hat, axis=0)  24.4 us
    ppermute x14, starting transfers between devices, tree_psum(): lax.ppermute(value, axis, pairs)  21.5 us
  transfers between devices with their start and end apart: 23, of which 14 were waited for; matrix products, arithmetic and copies ran while one was open for 25% of the time, Pallas kernels for 0%

profile of v1, /device:TPU:1, one launch (start us, length us, event | category | flops | bytes accessed | tf_op | source)
XLA Modules:
  0.0 725.4 jit_solution(7383191246290707501)
XLA Ops:
  7.2 6.5 copy.80
  13.7 3.1 multiply_reduce_fusion.3
  20.6 3.1 collective-permute-start.1
  25.3 3.9 collective-permute-start.2
  29.2 7.1 copy.81
  36.4 5.5 multiply_convert_fusion.2
  41.9 6.3 collective-permute-start.3
  48.9 6.5 fusion.10
  55.5 3.0 fusion.21
  60.4 4.5 convert_bitcast_fusion.3
  64.9 8.0 %copy.107 = bf16[32,512,128]{2,0,1:T(8,128)(2,1)} copy(bf16[32,512,128]{1,2,0:T(8,128)(2,1)} %convert_bitcast_fusion.3) | data formatting | bytes 8388608 | tf_op jit(solution)/shard_map/convert_element_type | solution.py:50
  72.9 6.3 all-to-all-start.2
  79.3 6.9 copy.82
  86.2 48.8 %all-to-all-done.2 = bf16[32,512,128]{2,0,1:T(8,128)(2,1)} async-done(((bf16[32,512,128]{2,0,1:T(8,128)(2,1)}), bf16[32,512,128]{2,0,1:T(8,128)(2,1)}, u32[]{:S(2)}, u32[]{:S(2)}) %all-to-all-start.2) | async-done | bytes 4194336 | tf_op jit(solution)/shard_map/all_to_all | solution.py:52
  135.0 4.9 all-to-all-start
  139.8 7.6 %copy.86 = bf16[512,32,128]{0,2,1:T(8,128)(2,1)} copy(bf16[512,32,128]{2,1,0:T(8,128)(2,1)} %param.12) | data formatting | bytes 8388608 | tf_op args[5]
  147.4 3.8 copy.108
  152.4 4.3 copy.109
  156.7 10.0 %copy.110 = f32[512,32,128]{0,2,1:T(8,128)} copy(f32[512,32,128]{2,1,0:T(8,128)} %bitcast.135) | data formatting | bytes 16777216 | tf_op jit(solution)/shard_map/convert_element_type | solution.py:54
  166.7 8.9 %convert_bitcast_fusion.2 = bf16[512,32,128]{0,2,1:T(8,128)(2,1)} fusion(bf16[512,512]{1,0:T(8,128)(2,1)S(1)} %copy-done, f32[512,32,128]{0,2,1:T(8,128)} %copy.110, bf16[512,32,128]{0,2,1:T(8,128)(2,1)} %copy.86), kind=kOutput, calls=%fused_computation.66 | convolution fusion | flops 2155872256 | bytes 17301504 | tf_op jit(solution)/shard_map/ijc,ik->kjc/dot_general | solution.py:55
  175.6 7.9 %copy.111 = bf16[512,32,128]{2,1,0:T(8,128)(2,1)} copy(bf16[512,32,128]{0,2,1:T(8,128)(2,1)} %convert_bitcast_fusion.2) | data formatting | bytes 8388608 | tf_op jit(solution)/shard_map/convert_element_type | solution.py:57
  183.5 12.0 %all-to-all-done = bf16[32,512,128]{2,0,1:T(8,128)(2,1)} async-done(((bf16[32,512,128]{2,0,1:T(8,128)(2,1)}), bf16[32,512,128]{2,0,1:T(8,128)(2,1)}, u32[]{:S(2)}, u32[]{:S(2)}) %all-to-all-start) | async-done | bytes 4194336 | tf_op jit(solution)/shard_map/all_to_all | solution.py:59
  195.6 5.5 all-to-all-start.3
  201.0 4.1 copy.84
  205.2 11.9 %fusion.29 = (bf16[512,32,128]{0,2,1:T(8,128)(2,1)}, bf16[512,32,128]{0,2,1:T(8,128)(2,1)S(1)}) fusion(f32[512,32,128]{0,2,1:T(8,128)} %copy.110, bf16[512,32,128]{0,2,1:T(8,128)(2,1)S(1)} %copy-done.3, bf16[512,512]{1,0:T(8,128)(2,1)S(1)} %copy-done, bf16[512,32,128]{2,1,0:T(8,128)(2,1)S(1)} %bitcast.133), kind=kOutput, calls=%fused_computation.53 | convolution fusion | flops 2157969408 | bytes 25690112 | tf_op jit(solution)/shard_map/kjc,ik->ijc/dot_general | solution.py:60
  217.1 7.6 %slice_bitcast_fusion = (bf16[1,32,32,128]{1,3,2,0:T(8,128)(2,1)}, bf16[1,32,32,128]{1,3,2,0:T(8,128)(2,1)}, bf16[1,32,32,128]{1,3,2,0:T(8,128)(2,1)}, bf16[1,32...) fusion(bf16[512,32,128]{0,2,1:T(8,128)(2,1)S(1)} %get-tuple-ele, ...), kind=kLoop, calls=%fused_computation.75 | loop fusion | bytes 8388608 | tf_op jit(solution)/shard_map/stack | solution.py:69
  233.2 2.4 copy.97
  235.5 2.4 copy.96
  237.9 2.4 copy.95
  242.7 2.4 copy.93
  249.8 2.4 copy.90
  277.5 5.7 all-to-all-start.1
  283.4 3.4 convert_bitcast_fusion
  286.8 4.3 copy.112
  291.1 47.9 %all-to-all-done.1 = bf16[16,32,32,128]{3,2,1,0:T(8,128)(2,1)} async-done(((bf16[16,32,32,128]{3,2,1,0:T(8,128)(2,1)}), bf16[16,32,32,128]{3,2,1,0:T(8,128)(2,1)}, u32[]{:S(2)}, u32[]{:S(2)}) %all-to-all-start.1) | async-done | bytes 4194336 | tf_op jit(solution)/shard_map/all_to_all | solution.py:68
  339.0 3.6 copy.103
  342.6 7.0 multiply_reduce_fusion
  349.7 9.0 %copy.105 = f32[32,512,128]{2,1,0:T(8,128)} copy(f32[32,512,128]{1,2,0:T(8,128)} %get-tuple-element.72) | data formatting | bytes 16777216 | tf_op jit(solution)/shard_map/ikc,jk->ijc/transpose | solution.py:75
  359.3 14.0 %fusion.22 = (f32[128]{0:T(128)S(1)}, f32[128]{0:T(128)S(1)}, f32[128]{0:T(128)S(1)}, f32[128]{0:T(128)S(1)}, f32[128]{0:T(128)S(1)}, /*index=5*/f32[16384,128]{1,0:T(8,128)S(1)}) fusion(bf16[16384,128]{1,0:T(8,128)(2,1)} %copy-done.4, bf16[2,128]{1,0:T(2,128)(2,1)S(1)} %collective-permute-done.3, bf16[16384,128]{1,0:T(8,128)(2,1)} %copy-done.7, ...), kind=kLoop, calls=%fused_computation.41 | loop fusion | flops 60816768 | bytes 37753344 | tf_op jit(solution)/shard_map/reduce_sum | solution.py:94
  373.3 2.5 collective-permute-start.5
  381.1 24.4 %multiply_reduce_fusion.1 = (f32[128]{0:T(128)S(1)}, f32[16384]{0:T(1024)S(1)}, f32[16384,128]{1,0:T(8,128)}) fusion(f32[32,512,128]{2,1,0:T(8,128)} %copy.81, f32[16384]{0:T(1024)S(1)} %add_rsqrt_fusion, f32[128]{0:T(128)S(1)} %copy-done.14, f32[2,128]{1,0:T(2,128)S(1)} %collective-permute-done.5, f32[16384,128]{1,0:T(8,128)} %copy-done.8, ...), kind=kLoop, calls=%fused_computation.57 | loop fusion | flops 44023680 | bytes 33691648 | tf_op jit(solution)/shard_map/reduce_sum | solution.py:96
  408.7 8.7 %fusion.35 = f32[512,512]{1,0:T(8,128)} fusion(bf16[512,32,128]{2,1,0:T(8,128)(2,1)} %bitcast.134, f32[512,32,128]{0,2,1:T(8,128)S(1)} %bitcast.130, bf16[512,32,128]{0,2,1:T(8,128)(2,1)} %copy.86), kind=kOutput, calls=%fused_computation.73 | convolution fusion | flops 2153775104 | bytes 17825792 | tf_op jit(solution)/shard_map/ijc,kjc->ik/dot_general | solution.py:65
  417.4 7.9 %copy.116 = bf16[512,32,128]{2,1,0:T(8,128)(2,1)} copy(bf16[512,32,128]{0,2,1:T(8,128)(2,1)} %get-tuple-element.47) | data formatting | bytes 8388608
  426.6 6.8 convolution_bitcast_fusion.1
  433.5 130.1 %all-reduce.3.cloned.1.call-done = f32[512,512]{1,0:T(8,128)} async-done(((f32[512,512]{1,0:T(8,128)}), f32[512,512]{1,0:T(8,128)}) %all-reduce.3.cloned.1.call-update) | async-done | bytes 1048592 | tf_op jit(solution)/shard_map/psum | solution.py:66
  574.8 2.4 collective-permute-start.8
  579.8 11.5 %multiply_convert_fusion.1 = bf16[16384,128]{1,0:T(8,128)(2,1)} fusion(f32[16384,128]{1,0:T(8,128)} %get-tuple-element.44, f32[32,512,128]{2,1,0:T(8,128)} %copy.81, f32[16384]{0:T(1024)S(1)} %add_multiply_fusion, f32[128]{0:T(128)S(1)} %copy-done.14, f32[16384]{0:T(1024)S(1)} %add_rsqrt_fusion), kind=kLoop, calls=%fused_computation.58 | loop fusion | flops 12582912 | bytes 21103104 | tf_op jit(solution)/shard_map/convert_element_type | solution.py:102
  591.3 124.7 %all-reduce.5.cloned.1.call-done = f32[512,512]{1,0:T(8,128)} async-done(((f32[512,512]{1,0:T(8,128)}), f32[512,512]{1,0:T(8,128)}) %all-reduce.5.cloned.1.call-update) | async-done | bytes 1048592 | tf_op jit(solution)/shard_map/psum | solution.py:80
  (124 shorter events, 76.9 us)
Async XLA Ops:
  7.2 159.5 %copy-start = (bf16[512,512]{1,0:T(8,128)(2,1)S(1)}, bf16[512,512]{1,0:T(8,128)(2,1)}, u32[]{:S(2)}) copy-start(bf16[512,512]{1,0:T(8,128)(2,1)} %param.11) | copy-start | bytes 1572868
  13.7 22.7 %copy-start.14 = (f32[128]{0:T(128)S(1)}, f32[128]{0:T(128)}, u32[]{:S(2)}) copy-start(f32[128]{0:T(128)} %param.8) | copy-start | bytes 1540
  16.8 3.8 collective-permute-start
  20.6 4.7 collective-permute-start.1
  25.3 11.0 %collective-permute-start.2 = (f32[16384]{0:T(1024)S(1)}, f32[16384]{0:T(1024)S(1)}, u32[]{:S(2)}, u32[]{:S(2)}) collective-permute-start(f32[16384]{0:T(1024)S(1)} %add.83), channel_id=1, source_target_pairs={{0,4},{1,5},{2,6},{3,7},{4,0},{5,1},{6,2},{7,3},{8,12},{9,13},{10,... | collective-permute-start | bytes 196616 | tf_op jit(solution)/shard_map/ppermute | solution.py:23
  36.3 11.9 %copy-start.15 = (f32[2,3,128]{2,0,1:T(2,128)S(1)}, f32[2,3,128]{2,0,1:T(2,128)}, u32[]{:S(2)}) copy-start(f32[2,3,128]{2,0,1:T(2,128)} %param.9) | copy-start | bytes 9220
  36.3 12.6 %copy-start.10 = (bf16[32,512,128]{2,1,0:T(8,128)(2,1)S(1)}, bf16[32,512,128]{2,1,0:T(8,128)(2,1)}, u32[]{:S(2)}) copy-start(bf16[32,512,128]{2,1,0:T(8,128)(2,1)} %param.13) | copy-start | bytes 12582916
  41.8 13.6 %copy-start.4 = (bf16[16384,128]{1,0:T(8,128)(2,1)}, bf16[16384,128]{1,0:T(8,128)(2,1)S(1)}, u32[]{:S(2)}) copy-start(bf16[16384,128]{1,0:T(8,128)(2,1)S(1)} %multiply_convert_fusion.2) | copy-start | bytes 12582916
  41.9 7.1 collective-permute-start.3
  55.5 3.0 copy-start.7
  55.5 5.0 copy-start.12
  58.5 1.9 copy-start.9
  72.9 62.0 %all-to-all-start.2 = ((bf16[32,512,128]{2,0,1:T(8,128)(2,1)}), bf16[32,512,128]{2,0,1:T(8,128)(2,1)}, u32[]{:S(2)}, u32[]{:S(2)}) async-start(bf16[32,512,128]{2,0,1:T(8,128)(2,1)} %copy.107), calls=%async_computation.2 | async-start | bytes 8388608 | tf_op jit(solution)/shard_map/all_to_all | solution.py:52
  135.0 60.6 %all-to-all-start = ((bf16[32,512,128]{2,0,1:T(8,128)(2,1)}), bf16[32,512,128]{2,0,1:T(8,128)(2,1)}, u32[]{:S(2)}, u32[]{:S(2)}) async-start(bf16[32,512,128]{2,0,1:T(8,128)(2,1)} %copy.82), calls=%async_computation | async-start | bytes 8388608 | tf_op jit(solution)/shard_map/all_to_all | solution.py:59
  195.6 81.9 %all-to-all-start.3 = ((bf16[512,32,128]{2,1,0:T(8,128)(2,1)}), bf16[512,32,128]{2,1,0:T(8,128)(2,1)}, u32[]{:S(2)}, u32[]{:S(2)}) async-start(bf16[512,32,128]{2,1,0:T(8,128)(2,1)} %copy.111), calls=%async_computation.3 | async-start | bytes 8388608 | tf_op jit(solution)/shard_map/all_to_all | solution.py:58
  201.0 4.1 copy-start.3
  205.1 12.0 %copy-start.5 = (bf16[16,32,32,128]{3,2,1,0:T(8,128)(2,1)}, bf16[16,32,32,128]{3,2,1,0:T(8,128)(2,1)S(1)}, u32[]{:S(2)}) copy-start(bf16[16,32,32,128]{3,2,1,0:T(8,128)(2,1)S(1)} %copy.84) | copy-start | bytes 12582916
  277.5 61.6 %all-to-all-start.1 = ((bf16[16,32,32,128]{3,2,1,0:T(8,128)(2,1)}), bf16[16,32,32,128]{3,2,1,0:T(8,128)(2,1)}, u32[]{:S(2)}, u32[]{:S(2)}) async-start(bf16[16,32,32,128]{3,2,1,0:T(8,128)(2,1)} %constant_dynamic-update-slice_fusion), calls=%async_computation.1 | async-start | bytes 8388608 | tf_op jit(solution)/shard_map/all_to_all | solution.py:68
  283.2 280.4 %all-reduce.3.cloned.1.call-start = ((), (), s32[]{:S(2)}) async-start(), calls=%async_computation.4 | async-start | bytes 2097152 | tf_op jit(solution)/shard_map/psum | solution.py:66
  291.1 51.5 %copy-start.13 = (bf16[512,512]{1,0:T(8,128)(2,1)S(1)}, bf16[512,512]{1,0:T(8,128)(2,1)}, u32[]{:S(2)}) copy-start(bf16[512,512]{1,0:T(8,128)(2,1)} %param.10) | copy-start | bytes 1572868
  339.0 3.6 copy-start.6
  342.6 7.1 copy-start.11
  359.3 21.7 %copy-start.2 = (f32[32,512,128]{2,1,0:T(8,128)S(1)}, f32[32,512,128]{2,1,0:T(8,128)}, u32[]{:S(2)}) copy-start(f32[32,512,128]{2,1,0:T(8,128)} %copy.105) | copy-start | bytes 25165828
  373.3 4.5 copy-start.8
  373.3 5.8 collective-permute-start.5
  375.8 5.3 collective-permute-start.4
  377.8 30.9 %slice-start = ((s8[8388608]{0:T(1024)(128)(4,1)}), s8[4194304]{0:T(1024)(128)(4,1)S(1)}, s32[]{:S(2)}) async-start(s8[8388608]{0:T(1024)(128)(4,1)} %bitcast.129), calls=%async_computation.6 | async-start | bytes 8388608
  377.8 30.9 %slice-start.1 = ((s8[8388608]{0:T(1024)(128)(4,1)}), s8[4194304]{0:T(1024)(128)(4,1)S(1)}, s32[]{:S(2)}) async-start(s8[8388608]{0:T(1024)(128)(4,1)} %bitcast.129), calls=%async_computation.7 | async-start | bytes 8388608
  405.5 1.2 collective-permute-start.9
  405.5 21.1 %collective-permute-start.13 = (f32[2,3,128]{2,1,0:T(4,128)S(1)}, f32[2,3,128]{2,1,0:T(4,128)S(1)}, u32[]{:S(2)}, u32[]{:S(2)}) collective-permute-start(f32[2,3,128]{2,1,0:T(4,128)S(1)} %pad_maximum_fusion.3), channel_id=1, source_target_pairs={{0,8},{8,0},{16,24},{24,16},{32,40},{40,32},{48,56},{56,48},{64,72... | collective-permute-start | bytes 9224 | tf_op jit(solution)/shard_map/ppermute | solution.py:23
  406.6 18.7 %collective-permute-start.10 = (f32[128]{0:T(128)S(1)}, f32[128]{0:T(128)S(1)}, u32[]{:S(2)}, u32[]{:S(2)}) collective-permute-start(f32[128]{0:T(128)S(1)} %add.100), channel_id=1, source_target_pairs={{0,16},{8,24},{16,0},{24,8},{32,48},{40,56},{48,32},{56,40},{64,80... | collective-permute-start | bytes 1544 | tf_op jit(solution)/shard_map/ppermute | solution.py:23
  417.4 298.6 %all-reduce.5.cloned.1.call-start = ((), (), s32[]{:S(2)}) async-start(), calls=%async_computation.5 | async-start | bytes 2097152 | tf_op jit(solution)/shard_map/psum | solution.py:80
  425.3 138.7 %collective-permute-start.11 = (f32[128]{0:T(128)S(1)}, f32[128]{0:T(128)S(1)}, u32[]{:S(2)}, u32[]{:S(2)}) collective-permute-start(f32[128]{0:T(128)S(1)} %add.101), channel_id=1, source_target_pairs={{0,32},{8,40},{16,48},{24,56},{32,0},{40,8},{48,16},{56,24},{64,96... | collective-permute-start | bytes 1544 | tf_op jit(solution)/shard_map/ppermute | solution.py:23
  426.5 138.4 %collective-permute-start.14 = (f32[2,3,128]{2,1,0:T(4,128)S(1)}, f32[2,3,128]{2,1,0:T(4,128)S(1)}, u32[]{:S(2)}, u32[]{:S(2)}) collective-permute-start(f32[2,3,128]{2,1,0:T(4,128)S(1)} %fusion.42), channel_id=1, source_target_pairs={{0,16},{8,24},{16,0},{24,8},{32,48},{40,56},{48,32},{56,40},{64,80... | collective-permute-start | bytes 9224 | tf_op jit(solution)/shard_map/ppermute | solution.py:23
  563.6 6.5 collective-permute-start.6
  564.1 8.1 %collective-permute-start.12 = (f32[128]{0:T(128)S(1)}, f32[128]{0:T(128)S(1)}, u32[]{:S(2)}, u32[]{:S(2)}) collective-permute-start(f32[128]{0:T(128)S(1)} %add.102), channel_id=1, source_target_pairs={{0,64},{8,72},{16,80},{24,88},{32,96},{40,104},{48,112},{56,120},{... | collective-permute-start | bytes 1544 | tf_op jit(solution)/shard_map/ppermute | solution.py:23
  564.9 4.0 collective-permute-start.15
  569.0 8.2 %collective-permute-start.16 = (f32[2,3,128]{2,1,0:T(4,128)S(1)}, f32[2,3,128]{2,1,0:T(4,128)S(1)}, u32[]{:S(2)}, u32[]{:S(2)}) collective-permute-start(f32[2,3,128]{2,1,0:T(4,128)S(1)} %add.106), channel_id=1, source_target_pairs={{0,64},{8,72},{16,80},{24,88},{32,96},{40,104},{48,112},{56,120},{... | collective-permute-start | bytes 9224 | tf_op jit(solution)/shard_map/ppermute | solution.py:23
  570.1 4.7 collective-permute-start.7
  574.8 5.0 collective-permute-start.8
  579.8 138.5 %copy-start.1 = (bf16[512,512]{1,0:T(8,128)(2,1)S(1)}, bf16[512,512]{1,0:T(8,128)(2,1)}, u32[]{:S(2)}) copy-start(bf16[512,512]{1,0:T(8,128)(2,1)} %param.11) | copy-start | bytes 1572868
Sparse Core Ops, SparseCore 0:
  417.5 146.0 all-reduce.2
  568.9 147.0 all-reduce.4
